TPU v7x, 512 devices: a whole 4x8x8 slice. The times are simulated.
512 devices in a mesh: context: 32 (over x_hi, y, core), tensor: 16 (over z, x_lo).
Axes of the slice: x: 4 (x_hi: 2, x_lo: 2; x = x_hi * 2 + x_lo), y: 8, z: 8, core: 2. Of those that a mesh axis runs over, the one named last changes fastest.
Arguments:
- projected: bfloat16 [3, 12288, 8192], P(None, 'context', 'tensor'), may hold values from -6 to 6
- taps: float32 [3, 3, 8192], P(None, None, 'tensor'), may hold values from -4 to 4
- filters: bfloat16 [512, 128], P('tensor'), may hold values from -0.5 to 0.5
- skip: float32 [8192], P('tensor'), may hold values from -4 to 4
- out_weight: bfloat16 [8192, 8192], P('tensor', 'context'), may hold values from -0.125 to 0.125
- positions: int32 [128], replicated, may hold values from 0 to 12287
Outputs:
- mixed: bfloat16 [12288, 8192], P('context', 'tensor')
- variant_states: bfloat16 [128, 8192], P('context', 'tensor')
All inputs are finite; a program needn't handle non-finite values.
Results may differ from a plain program's by a relative error of at most 0.018.
Values may be sent and summed in bfloat16 or wider, within the bound.
No kernel may reach another device: no remote copies, remote signals or barrier semaphores. Data moves between devices by JAX's collectives and lax.ppermute only.
A program may use at most 128 MiB of HBM per device.

v0:
```python
import jax
import jax.numpy as jnp
from jax import lax
from jax.sharding import PartitionSpec as P

FLT = 128
GROUP = 16
SHORT = 3


def shifted(array, axis, by):
    size = lax.axis_size(axis)
    pairs = [(i, i + by) for i in range(size) if 0 <= i + by < size]
    return lax.ppermute(array, axis, pairs)


def halving_scatter(rows, axis):
    size = lax.axis_size(axis)
    if size & size - 1 or rows.shape[0] % size:
        return lax.psum_scatter(rows, axis, scatter_dimension=0, tiled=True)
    me = lax.axis_index(axis)
    step = size // 2
    while step >= 1:
        half = rows.shape[0] // 2
        bit = me // step % 2
        keep = lax.dynamic_slice_in_dim(rows, bit * half, half, 0)
        send = lax.dynamic_slice_in_dim(rows, (1 - bit) * half, half, 0)
        pairs = [(i, i ^ step) for i in range(size)]
        rows = keep + lax.ppermute(send, axis, pairs)
        step //= 2
    return rows


def short_filter(extended, weights, count):
    lags = SHORT - 1
    total = jnp.zeros((extended.shape[0], count, extended.shape[2]), jnp.float32)
    for lag in range(SHORT):
        total = total + weights[:, lag, None, :] * extended[
            :, lags - lag : lags - lag + count, :
        ].astype(jnp.float32)
    return total


def banded_filters(filters, rows):
    local_groups = filters.shape[0]
    span = FLT - 1 + rows
    reversed_taps = jnp.flip(filters, axis=1)
    padded_taps = jnp.concatenate(
        [reversed_taps, jnp.zeros((local_groups, rows), filters.dtype)], axis=1
    )
    tiled = jnp.tile(padded_taps, (1, rows))
    return tiled[:, : rows * span].reshape(local_groups, rows, span)


def on_device(projected, taps, filters, skip, out_weight, positions):
    rows = projected.shape[1]
    width = projected.shape[2]
    lags = SHORT - 1
    reach = FLT - 1
    rim = shifted(projected[:, rows - lags :, :], "context", 1)
    feat = short_filter(jnp.concatenate([rim, projected], axis=1), taps, rows)
    query = feat[0]
    product = (feat[1] * feat[2]).astype(jnp.bfloat16)
    prior = shifted(product[rows - reach :], "context", 1)
    extended = jnp.concatenate([prior, product], axis=0)
    span = reach + rows
    toeplitz = banded_filters(filters, rows)
    local_groups = filters.shape[0]
    conv = jnp.einsum(
        "gim,mgc->igc",
        toeplitz,
        extended.reshape(span, local_groups, GROUP),
        preferred_element_type=jnp.float32,
    ).reshape(rows, width)
    conv = conv + skip[None, :] * product.astype(jnp.float32)
    gated = (query * conv).astype(jnp.bfloat16)
    terms = jnp.dot(
        gated,
        lax.all_gather(out_weight, "context", axis=1, tiled=True),
        preferred_element_type=jnp.float32,
    )
    mixed = lax.psum_scatter(terms.astype(jnp.bfloat16), "tensor", scatter_dimension=1, tiled=True)
    offset = lax.axis_index("context") * rows
    local_sites = positions - offset
    one_hot = (local_sites[:, None] == jnp.arange(rows, dtype=jnp.int32)[None, :]).astype(
        jnp.bfloat16
    )
    picked_terms = jnp.dot(one_hot, mixed, preferred_element_type=jnp.float32)
    variant_states = halving_scatter(picked_terms.astype(jnp.bfloat16), "context")
    return (mixed, variant_states)


def solution(mesh):
    return jax.shard_map(
        on_device,
        mesh=mesh,
        in_specs=(
            P(None, "context", "tensor"),
            P(None, None, "tensor"),
            P("tensor", None),
            P("tensor"),
            P("tensor", "context"),
            P(),
        ),
        out_specs=(P("context", "tensor"), P("context", "tensor")),
        check_vma=False,
    )
```

profile of v0, /device:TPU:1, one launch (start us, length us, event | category | flops | bytes accessed | tf_op | source)
XLA Modules:
  0.0 321.8 jit_solution(6811182927905983735)
XLA Ops:
  7.2 0.0 all-gather.2.cloned.1.call-start
  7.2 0.7 all-gather.2.cloned.1.call-update
  7.9 0.0 reduce-scatter.2.cloned.1.call-start
  7.9 0.8 slice.38
  8.7 4.6 %collective-permute-start = (bf16[3,2,512]{2,1,0:T(2,128)(2,1)S(1)}, bf16[3,2,512]{2,1,0:T(2,128)(2,1)S(1)}, u32[]{:S(2)}, u32[]{:S(2)}) collective-permute-start(bf16[3,2,512]{2,1,0:T(2,128)(2,1)S(1)} %slice.38), channel_id=1, source_target_pairs={{0,16},{16,32},{32,48},{48,64},{64,80},{80,96},{96,112},{112,128},... | collective-permute-start | bytes 18440 | tf_op jit(solution)/shard_map/ppermute | solution.py:14
  13.3 0.9 fusion.8
  14.2 0.6 copy.19
  14.8 0.8 rev.4
  15.6 5.4 %tile.4 = bf16[32,384,512]{2,1,0:T(8,128)(2,1)} broadcast(bf16[32,512]{1,0:T(8,128)(2,1)S(1)} %concatenate.11), dimensions={0,2} | broadcast | bytes 12615680 | tf_op jit(solution)/shard_map/tile | solution.py:51
  21.0 12.0 %copy.15 = bf16[4,8,384,512]{3,1,2,0:T(8,128)(2,1)S(1)} copy(bf16[4,8,384,512]{3,2,1,0:T(8,128)(2,1)} %bitcast.32) | data formatting | bytes 25165824
  33.0 5.1 %slice.54 = bf16[32,196224]{1,0:T(8,128)(2,1)} slice(bf16[32,196608]{1,0:T(8,128)(2,1)S(1)} %bitcast.33), slice={[0:32], [0:196224]} | slice | bytes 25116672 | tf_op jit(solution)/shard_map/slice | solution.py:52
  38.2 0.0 copy-start
  38.2 29.3 %reshape.23 = bf16[32,384,511]{2,1,0:T(8,128)(2,1)} reshape(bf16[32,196224]{1,0:T(8,128)(2,1)} %slice.54) | data formatting | bytes 25116672 | tf_op jit(solution)/shard_map/reshape | solution.py:52
  67.5 0.0 collective-permute-done
  67.5 0.0 copy-start.1
  67.5 0.6 copy-done.1
  68.1 0.0 copy-done
  68.1 1.5 multiply_add_fusion
  69.6 0.1 fusion.1
  69.8 2.1 collective-permute-start.1
  71.9 0.1 fusion.14
  72.0 3.4 %collective-permute-done.1 = bf16[127,512]{1,0:T(8,128)(2,1)S(1)} collective-permute-done((bf16[127,512]{1,0:T(8,128)(2,1)S(1)}, bf16[127,512]{1,0:T(8,128)(2,1)S(1)}, u32[]{:S(2)}, u32[]{:S(2)}) %collective-permute-start.1) | collective-permute-done | bytes 130080 | tf_op jit(solution)/shard_map/ppermute | solution.py:14
  75.5 0.1 pad_maximum_fusion.1
  75.5 1.0 copy.10
  76.6 0.0 copy-start.2
  76.6 8.3 %fusion.9 = f32[32,16,384]{2,1,0:T(8,128)S(1)} fusion(bf16[511,32,16]{0,2,1:T(8,128)(2,1)} %bitcast.35, bf16[32,384,511]{2,1,0:T(8,128)(2,1)} %reshape.23), kind=kOutput, calls=%fused_computation.33 | convolution fusion | flops 200933376 | bytes 13868032 | tf_op jit(solution)/shard_map/gim,mgc->igc/dot_general | solution.py:69
  84.9 1.2 copy.11
  86.1 44.6 %all-gather.2.cloned.1.call-done = bf16[512,8192]{1,0:T(8,128)(2,1)} async-done(((bf16[512,256]{1,0:T(8,128)(2,1)}), bf16[512,8192]{1,0:T(8,128)(2,1)}) %all-gather.2.cloned.1.call-update) | async-done | bytes 8388624 | tf_op jit(solution)/shard_map/all_gather | solution.py:79
  130.7 0.0 copy-done.2
  130.7 9.8 %convolution_convert_fusion = bf16[384,8192]{1,0:T(8,128)(2,1)} fusion(bf16[512,8192]{1,0:T(8,128)(2,1)} %all-gather.2.cloned.1.call-done, f32[3,384,512]{2,1,0:T(8,128)S(1)} %multiply_add_fusion, f32[384,512]{1,0:T(8,128)} %copy.11, f32[512]{0:T(512)S(1)} %copy-done.2, bf16[1,384,512]{2,1,0:T(8,128)(2,1)S(1)} %fusion.1), kind=kOutput, calls=%fused_computation | convolution fusion | flops 3225354240 | bytes 16648192 | tf_op jit(solution)/shard_map/dot_general | solution.py:77
  140.5 0.0 copy-start.3
  140.5 0.0 reduce-scatter.2.cloned.1.call-update
  140.5 0.6 copy-done.3
  141.1 138.4 %reduce-scatter.2.cloned.1.call-done = bf16[384,512]{1,0:T(8,128)(2,1)} async-done(((bf16[384,8192]{1,0:T(8,128)(2,1)}), bf16[384,512]{1,0:T(8,128)(2,1)}) %reduce-scatter.2.cloned.1.call-update) | async-done | bytes 393232 | tf_op jit(solution)/shard_map/reduce_scatter | solution.py:82
  279.6 1.3 convolution_convert_fusion.1
  280.8 4.7 %collective-permute-start.2 = (bf16[64,512]{1,0:T(8,128)(2,1)S(1)}, bf16[64,512]{1,0:T(8,128)(2,1)S(1)}, u32[]{:S(2)}, u32[]{:S(2)}) collective-permute-start(bf16[64,512]{1,0:T(8,128)(2,1)S(1)} %constant_dynamic-slice_fusion.4), channel_id=1, source_target_pairs={{0,256},{16,272},{32,288},{48,304},{64,320},{80,336},{96,352},{112... | collective-permute-start | bytes 196616 | tf_op jit(solution)/shard_map/ppermute | solution.py:29
  285.6 1.7 collective-permute-done.2
  287.4 7.2 %collective-permute-start.3 = (bf16[32,512]{1,0:T(8,128)(2,1)S(1)}, bf16[32,512]{1,0:T(8,128)(2,1)S(1)}, u32[]{:S(2)}, u32[]{:S(2)}) collective-permute-start(bf16[32,512]{1,0:T(8,128)(2,1)S(1)} %constant_dynamic-slice_fusion.3), channel_id=1, source_target_pairs={{0,128},{16,144},{32,160},{48,176},{64,192},{80,208},{96,224},{112... | collective-permute-start | bytes 98312 | tf_op jit(solution)/shard_map/ppermute | solution.py:29
  294.7 1.3 collective-permute-done.3
  296.0 4.4 %collective-permute-start.4 = (bf16[16,512]{1,0:T(8,128)(2,1)S(1)}, bf16[16,512]{1,0:T(8,128)(2,1)S(1)}, u32[]{:S(2)}, u32[]{:S(2)}) collective-permute-start(bf16[16,512]{1,0:T(8,128)(2,1)S(1)} %constant_dynamic-slice_fusion.2), channel_id=1, source_target_pairs={{0,64},{16,80},{32,96},{48,112},{64,0},{80,16},{96,32},{112,48},{1... | collective-permute-start | bytes 49160 | tf_op jit(solution)/shard_map/ppermute | solution.py:29
  300.5 1.1 collective-permute-done.4
  301.6 3.0 collective-permute-start.5
  304.7 1.3 collective-permute-done.5
  306.0 7.5 %collective-permute-start.6 = (bf16[4,512]{1,0:T(4,128)(2,1)S(1)}, bf16[4,512]{1,0:T(4,128)(2,1)S(1)}, u32[]{:S(2)}, u32[]{:S(2)}) collective-permute-start(bf16[4,512]{1,0:T(4,128)(2,1)S(1)} %constant_dynamic-slice_fusion), channel_id=1, source_target_pairs={{0,16},{16,0},{32,48},{48,32},{64,80},{80,64},{96,112},{112,96},{1... | collective-permute-start | bytes 12296 | tf_op jit(solution)/shard_map/ppermute | solution.py:29
  313.5 0.8 collective-permute-done.6
  314.3 0.6 dynamic-slice_add_fusion.4
  (13 shorter events, 0.1 us)
Async XLA Ops:
  7.2 123.5 %all-gather.2.cloned.1.call-start = ((), (), s32[]{:S(2)}) async-start(), calls=%async_computation.1 | async-start | bytes 8650752 | tf_op jit(solution)/shard_map/all_gather | solution.py:79
  7.9 271.7 %reduce-scatter.2.cloned.1.call-start = ((), (), s32[]{:S(2)}) async-start(), calls=%async_computation.2 | async-start | bytes 6684672 | tf_op jit(solution)/shard_map/reduce_scatter | solution.py:82
  8.7 58.8 %collective-permute-start = (bf16[3,2,512]{2,1,0:T(2,128)(2,1)S(1)}, bf16[3,2,512]{2,1,0:T(2,128)(2,1)S(1)}, u32[]{:S(2)}, u32[]{:S(2)}) collective-permute-start(bf16[3,2,512]{2,1,0:T(2,128)(2,1)S(1)} %slice.38), channel_id=1, source_target_pairs={{0,16},{16,32},{32,48},{48,64},{64,80},{80,96},{96,112},{112,128},... | collective-permute-start | bytes 18440 | tf_op jit(solution)/shard_map/ppermute | solution.py:14
  38.2 29.9 %copy-start = (bf16[3,384,512]{2,1,0:T(8,128)(2,1)S(1)}, bf16[3,384,512]{2,1,0:T(8,128)(2,1)}, u32[]{:S(2)}) copy-start(bf16[3,384,512]{2,1,0:T(8,128)(2,1)} %param.6) | copy-start | bytes 3538948
  67.5 0.6 copy-start.1
  69.8 5.7 %collective-permute-start.1 = (bf16[127,512]{1,0:T(8,128)(2,1)S(1)}, bf16[127,512]{1,0:T(8,128)(2,1)S(1)}, u32[]{:S(2)}, u32[]{:S(2)}) collective-permute-start(bf16[127,512]{1,0:T(8,128)(2,1)S(1)} %slice_bitcast_fusion.1), channel_id=1, source_target_pairs={{0,16},{16,32},{32,48},{48,64},{64,80},{80,96},{96,112},{112,128},... | collective-permute-start | bytes 390152 | tf_op jit(solution)/shard_map/ppermute | solution.py:14
  76.6 54.1 %copy-start.2 = (f32[512]{0:T(512)S(1)}, f32[512]{0:T(512)}, u32[]{:S(2)}) copy-start(f32[512]{0:T(512)} %param.9) | copy-start | bytes 6148
  140.5 0.7 copy-start.3
  280.8 6.5 %collective-permute-start.2 = (bf16[64,512]{1,0:T(8,128)(2,1)S(1)}, bf16[64,512]{1,0:T(8,128)(2,1)S(1)}, u32[]{:S(2)}, u32[]{:S(2)}) collective-permute-start(bf16[64,512]{1,0:T(8,128)(2,1)S(1)} %constant_dynamic-slice_fusion.4), channel_id=1, source_target_pairs={{0,256},{16,272},{32,288},{48,304},{64,320},{80,336},{96,352},{112... | collective-permute-start | bytes 196616 | tf_op jit(solution)/shard_map/ppermute | solution.py:29
  287.4 8.6 %collective-permute-start.3 = (bf16[32,512]{1,0:T(8,128)(2,1)S(1)}, bf16[32,512]{1,0:T(8,128)(2,1)S(1)}, u32[]{:S(2)}, u32[]{:S(2)}) collective-permute-start(bf16[32,512]{1,0:T(8,128)(2,1)S(1)} %constant_dynamic-slice_fusion.3), channel_id=1, source_target_pairs={{0,128},{16,144},{32,160},{48,176},{64,192},{80,208},{96,224},{112... | collective-permute-start | bytes 98312 | tf_op jit(solution)/shard_map/ppermute | solution.py:29
  296.0 5.5 %collective-permute-start.4 = (bf16[16,512]{1,0:T(8,128)(2,1)S(1)}, bf16[16,512]{1,0:T(8,128)(2,1)S(1)}, u32[]{:S(2)}, u32[]{:S(2)}) collective-permute-start(bf16[16,512]{1,0:T(8,128)(2,1)S(1)} %constant_dynamic-slice_fusion.2), channel_id=1, source_target_pairs={{0,64},{16,80},{32,96},{48,112},{64,0},{80,16},{96,32},{112,48},{1... | collective-permute-start | bytes 49160 | tf_op jit(solution)/shard_map/ppermute | solution.py:29
  301.6 4.4 %collective-permute-start.5 = (bf16[8,512]{1,0:T(8,128)(2,1)S(1)}, bf16[8,512]{1,0:T(8,128)(2,1)S(1)}, u32[]{:S(2)}, u32[]{:S(2)}) collective-permute-start(bf16[8,512]{1,0:T(8,128)(2,1)S(1)} %constant_dynamic-slice_fusion.1), channel_id=1, source_target_pairs={{0,32},{16,48},{32,0},{48,16},{64,96},{80,112},{96,64},{112,80},{1... | collective-permute-start | bytes 24584 | tf_op jit(solution)/shard_map/ppermute | solution.py:29
  306.0 8.3 %collective-permute-start.6 = (bf16[4,512]{1,0:T(4,128)(2,1)S(1)}, bf16[4,512]{1,0:T(4,128)(2,1)S(1)}, u32[]{:S(2)}, u32[]{:S(2)}) collective-permute-start(bf16[4,512]{1,0:T(4,128)(2,1)S(1)} %constant_dynamic-slice_fusion), channel_id=1, source_target_pairs={{0,16},{16,0},{32,48},{48,32},{64,80},{80,64},{96,112},{112,96},{1... | collective-permute-start | bytes 12296 | tf_op jit(solution)/shard_map/ppermute | solution.py:29
Sparse Core Ops, SparseCore 0:
  11.1 119.4 all-gather.1
  140.6 138.9 reduce-scatter.1
where the time goes:
time: 322 us
  waiting for transfers between devices  193 us (60%)
  local copies, waits for them, and re-layouts  58.4 us (18%)
  starting transfers between devices  33.7 us (10%)
  matrix products  19.4 us (6%)
  between operations  14.4 us (4%)
    reduce_scatter x1, waiting for transfers between devices, on_device(): lax.psum_scatter(terms.astype(jnp.bfloat16), 'tensor', scatter_dimension=...  138 us
    all_gather x1, waiting for transfers between devices, on_device(): lax.all_gather(out_weight, 'context', axis=1, tiled=True)  44.6 us
    reshape x1, local copies, waits for them, and re-layouts, banded_filters(): return tiled[:, :rows * span].reshape(local_groups, rows, span)  29.3 us
    ppermute x5, starting transfers between devices, halving_scatter(): rows = keep + lax.ppermute(send, axis, pairs)  26.9 us
    unnamed x11, local copies, waits for them, and re-layouts  13.8 us
    dot_general x1, matrix products, on_device(): jnp.dot(gated, lax.all_gather(out_weight, 'context', axis=1, tiled=True),...  9.78 us
    dot_general x1, matrix products, on_device(): jnp.einsum('gim,mgc->igc', toeplitz, extended.reshape(span, local_groups,...  8.33 us
    ppermute x2, starting transfers between devices, shifted(): return lax.ppermute(array, axis, pairs)  6.72 us
  transfers between devices with their start and end apart: 9, of which 8 were waited for; matrix products, arithmetic and copies ran while one was open for 21% of the time, Pallas kernels for 0%

commit v1 on v0

--- a/solution.py
+++ b/solution.py
@@ -76,7 +76,10 @@
     gated = (query * conv).astype(jnp.bfloat16)
     terms = jnp.dot(
         gated,
-        lax.all_gather(out_weight, "context", axis=1, tiled=True),
+        jnp.concatenate(
+            lax.all_to_all(jnp.stack([out_weight] * lax.axis_size("context")), "context", 0, 0),
+            axis=1,
+        ),
         preferred_element_type=jnp.float32,
     )
     mixed = lax.psum_scatter(terms.astype(jnp.bfloat16), "tensor", scatter_dimension=1, tiled=True)

time: 322 us -> 425 us (1.32)
  waiting for transfers between devices: 193 us -> 280 us
  starting transfers between devices: 33.7 us -> 47.1 us
    ppermute x2, waiting for transfers between devices: 3.45 us -> 125 us  [shifted(): return lax.ppermute(array, axis, pairs)]
    all_gather x1 -> x0, waiting for transfers between devices: 44.6 us -> none  [on_device(): lax.all_gather(out_weight, 'context', axis=1, tiled=True)]
    all_to_all x0 -> x1, starting transfers between devices: none -> 11.5 us  [on_device(): lax.all_to_all(jnp.stack([out_weight] * lax.axis_size('context')), 'conte...]
    reduce_scatter x1, waiting for transfers between devices: 138 us -> 148 us  [on_device(): lax.psum_scatter(terms.astype(jnp.bfloat16), 'tensor', scatter_dimension=...]
    unnamed x11 -> x16, local copies, waits for them, and re-layouts: 13.8 us -> 14.9 us
  transfers between devices with their start and end apart: 9 -> 9, of which waited for: 8 -> 8; matrix products, arithmetic and copies ran while one was open for 21% -> 15% of each run, Pallas kernels for 0% -> 0%
where the time goes in v1:
time: 425 us; the launch traced here: 424 us
  waiting for transfers between devices  280 us (66%)
  local copies, waits for them, and re-layouts  61.3 us (14%)
  starting transfers between devices  47.1 us (11%)
  matrix products  19.2 us (5%)
  between operations  14.4 us (3%)
    reduce_scatter x1, waiting for transfers between devices, on_device(): lax.psum_scatter(terms.astype(jnp.bfloat16), 'tensor', scatter_dimension=...  148 us
    ppermute x2, waiting for transfers between devices, shifted(): return lax.ppermute(array, axis, pairs)  125 us
    reshape x1, local copies, waits for them, and re-layouts, banded_filters(): return tiled[:, :rows * span].reshape(local_groups, rows, span)  29.2 us
    ppermute x5, starting transfers between devices, halving_scatter(): rows = keep + lax.ppermute(send, axis, pairs)  27.1 us
    unnamed x16, local copies, waits for them, and re-layouts  14.9 us
    all_to_all x1, starting transfers between devices, on_device(): lax.all_to_all(jnp.stack([out_weight] * lax.axis_size('context')), 'conte...  11.5 us
    dot_general x1, matrix products, on_device(): jnp.dot(gated, jnp.concatenate(lax.all_to_all(jnp.stack([out_weight] * la...  9.81 us
  transfers between devices with their start and end apart: 9, of which 8 were waited for; matrix products, arithmetic and copies ran while one was open for 15% of the time, Pallas kernels for 0%

profile of v1, /device:TPU:1, one launch (start us, length us, event | category | flops | bytes accessed | tf_op | source)
XLA Modules:
  0.0 424.5 jit_solution(11406022080838254581)
XLA Ops:
  7.2 1.1 copy.12
  8.3 4.2 stack.2
  12.5 0.0 copy-start
  12.5 0.0 copy-start.1
  12.5 0.0 copy-start.2
  12.5 11.5 %all-to-all-start = ((bf16[32,512,256]{1,2,0:T(8,128)(2,1)}), bf16[32,512,256]{1,2,0:T(8,128)(2,1)}, u32[]{:S(2)}, u32[]{:S(2)}) async-start(bf16[32,512,256]{1,2,0:T(8,128)(2,1)} %stack.2), calls=%async_computation | async-start | bytes 16777216 | tf_op jit(solution)/shard_map/all_to_all | solution.py:80
  24.0 0.0 reduce-scatter.2.cloned.1.call-start
  24.1 0.0 copy-done
  24.1 3.5 collective-permute-start
  27.6 0.0 copy-done.1
  27.7 0.6 copy.20
  28.3 0.0 copy-done.2
  28.3 0.1 rev.4
  28.4 5.5 %tile.4 = bf16[32,384,512]{2,1,0:T(8,128)(2,1)} broadcast(bf16[32,512]{1,0:T(8,128)(2,1)S(1)} %concatenate.11), dimensions={0,2} | broadcast | bytes 12615680 | tf_op jit(solution)/shard_map/tile | solution.py:51
  33.9 12.0 %copy.16 = bf16[4,8,384,512]{3,1,2,0:T(8,128)(2,1)S(1)} copy(bf16[4,8,384,512]{3,2,1,0:T(8,128)(2,1)} %bitcast.27) | data formatting | bytes 25165824
  45.9 5.1 %slice.54 = bf16[32,196224]{1,0:T(8,128)(2,1)} slice(bf16[32,196608]{1,0:T(8,128)(2,1)S(1)} %bitcast.28), slice={[0:32], [0:196224]} | slice | bytes 25116672 | tf_op jit(solution)/shard_map/slice | solution.py:52
  51.0 29.2 %reshape.39 = bf16[32,384,511]{2,1,0:T(8,128)(2,1)} reshape(bf16[32,196224]{1,0:T(8,128)(2,1)} %slice.54) | data formatting | bytes 25116672 | tf_op jit(solution)/shard_map/reshape | solution.py:52
  80.2 123.9 %collective-permute-done = bf16[3,2,512]{2,1,0:T(2,128)(2,1)S(1)} collective-permute-done((bf16[3,2,512]{2,1,0:T(2,128)(2,1)S(1)}, bf16[3,2,512]{2,1,0:T(2,128)(2,1)S(1)}, u32[]{:S(2)}, u32[]{:S(2)}) %collective-permute-start) | collective-permute-done | bytes 6176 | tf_op jit(solution)/shard_map/ppermute | solution.py:14
  204.1 0.0 copy-start.3
  204.1 0.6 copy-done.3
  204.7 1.5 multiply_add_fusion
  206.2 0.1 fusion.1
  206.4 4.9 %collective-permute-start.1 = (bf16[127,512]{1,0:T(8,128)(2,1)S(1)}, bf16[127,512]{1,0:T(8,128)(2,1)S(1)}, u32[]{:S(2)}, u32[]{:S(2)}) collective-permute-start(bf16[127,512]{1,0:T(8,128)(2,1)S(1)} %slice_bitcast_fusion), channel_id=1, source_target_pairs={{0,16},{16,32},{32,48},{48,64},{64,80},{80,96},{96,112},{112,128},... | collective-permute-start | bytes 390152 | tf_op jit(solution)/shard_map/ppermute | solution.py:14
  211.3 0.1 fusion.13
  211.4 1.6 collective-permute-done.1
  213.0 0.1 pad_maximum_fusion.1
  213.1 1.1 copy.10
  214.2 0.0 copy-start.4
  214.2 8.1 %fusion.8 = f32[32,16,384]{2,1,0:T(8,128)S(1)} fusion(bf16[511,32,16]{0,2,1:T(8,128)(2,1)} %bitcast.30, bf16[32,384,511]{2,1,0:T(8,128)(2,1)} %reshape.39), kind=kOutput, calls=%fused_computation.32 | convolution fusion | flops 200933376 | bytes 13868032 | tf_op jit(solution)/shard_map/gim,mgc->igc/dot_general | solution.py:69
  222.3 1.2 copy.11
  223.5 0.0 all-to-all-done
  223.5 0.0 copy-done.4
  223.5 9.8 %convolution_convert_fusion = bf16[384,8192]{1,0:T(8,128)(2,1)} fusion(bf16[512,8192]{0,1:T(8,128)(2,1)} %bitcast.7, f32[1,384,512]{2,1,0:T(8,128)} %copy.11, bf16[1,384,512]{2,1,0:T(8,128)(2,1)S(1)} %fusion.1, f32[3,384,512]{2,1,0:T(8,128)S(1)} %multiply_add_fusion, f32[512]{0:T(512)S(1)} %copy-done.4), kind=kOutput, calls=%fused_computation | convolution fusion | flops 3225354240 | bytes 16648192 | tf_op jit(solution)/shard_map/dot_general | solution.py:77
  233.3 0.0 reduce-scatter.2.cloned.1.call-update
  233.3 0.6 copy-done.5
  233.9 148.2 %reduce-scatter.2.cloned.1.call-done = bf16[384,512]{1,0:T(8,128)(2,1)} async-done(((bf16[384,8192]{1,0:T(8,128)(2,1)}), bf16[384,512]{1,0:T(8,128)(2,1)}) %reduce-scatter.2.cloned.1.call-update) | async-done | bytes 393232 | tf_op jit(solution)/shard_map/reduce_scatter | solution.py:85
  382.1 1.3 convolution_convert_fusion.1
  383.4 4.8 %collective-permute-start.2 = (bf16[64,512]{1,0:T(8,128)(2,1)S(1)}, bf16[64,512]{1,0:T(8,128)(2,1)S(1)}, u32[]{:S(2)}, u32[]{:S(2)}) collective-permute-start(bf16[64,512]{1,0:T(8,128)(2,1)S(1)} %constant_dynamic-slice_fusion.4), channel_id=1, source_target_pairs={{0,256},{16,272},{32,288},{48,304},{64,320},{80,336},{96,352},{112... | collective-permute-start | bytes 196616 | tf_op jit(solution)/shard_map/ppermute | solution.py:29
  388.2 1.7 collective-permute-done.2
  390.0 7.2 %collective-permute-start.3 = (bf16[32,512]{1,0:T(8,128)(2,1)S(1)}, bf16[32,512]{1,0:T(8,128)(2,1)S(1)}, u32[]{:S(2)}, u32[]{:S(2)}) collective-permute-start(bf16[32,512]{1,0:T(8,128)(2,1)S(1)} %constant_dynamic-slice_fusion.3), channel_id=1, source_target_pairs={{0,128},{16,144},{32,160},{48,176},{64,192},{80,208},{96,224},{112... | collective-permute-start | bytes 98312 | tf_op jit(solution)/shard_map/ppermute | solution.py:29
  397.3 1.3 collective-permute-done.3
  398.6 4.4 %collective-permute-start.4 = (bf16[16,512]{1,0:T(8,128)(2,1)S(1)}, bf16[16,512]{1,0:T(8,128)(2,1)S(1)}, u32[]{:S(2)}, u32[]{:S(2)}) collective-permute-start(bf16[16,512]{1,0:T(8,128)(2,1)S(1)} %constant_dynamic-slice_fusion.2), channel_id=1, source_target_pairs={{0,64},{16,80},{32,96},{48,112},{64,0},{80,16},{96,32},{112,48},{1... | collective-permute-start | bytes 49160 | tf_op jit(solution)/shard_map/ppermute | solution.py:29
  403.1 1.1 collective-permute-done.4
  404.2 3.1 collective-permute-start.5
  407.3 1.3 collective-permute-done.5
  408.6 7.6 %collective-permute-start.6 = (bf16[4,512]{1,0:T(4,128)(2,1)S(1)}, bf16[4,512]{1,0:T(4,128)(2,1)S(1)}, u32[]{:S(2)}, u32[]{:S(2)}) collective-permute-start(bf16[4,512]{1,0:T(4,128)(2,1)S(1)} %constant_dynamic-slice_fusion), channel_id=1, source_target_pairs={{0,16},{16,0},{32,48},{48,32},{64,80},{80,64},{96,112},{112,96},{1... | collective-permute-start | bytes 12296 | tf_op jit(solution)/shard_map/ppermute | solution.py:29
  416.2 0.8 collective-permute-done.6
  417.0 0.6 dynamic-slice_add_fusion.4
  (16 shorter events, 0.2 us)
Async XLA Ops:
  12.5 11.6 %copy-start = (bf16[3,384,512]{2,1,0:T(8,128)(2,1)S(1)}, bf16[3,384,512]{2,1,0:T(8,128)(2,1)}, u32[]{:S(2)}) copy-start(bf16[3,384,512]{2,1,0:T(8,128)(2,1)} %param.6) | copy-start | bytes 3538948
  12.5 15.2 %copy-start.1 = (f32[3,3,512]{2,1,0:T(4,128)S(1)}, f32[3,3,512]{2,1,0:T(4,128)}, u32[]{:S(2)}) copy-start(f32[3,3,512]{2,1,0:T(4,128)} %param.7) | copy-start | bytes 55300
  12.5 15.8 %copy-start.2 = (bf16[32,128]{1,0:T(8,128)(2,1)S(1)}, bf16[32,128]{1,0:T(8,128)(2,1)}, u32[]{:S(2)}) copy-start(bf16[32,128]{1,0:T(8,128)(2,1)} %param.8) | copy-start | bytes 24580
  12.5 211.0 %all-to-all-start = ((bf16[32,512,256]{1,2,0:T(8,128)(2,1)}), bf16[32,512,256]{1,2,0:T(8,128)(2,1)}, u32[]{:S(2)}, u32[]{:S(2)}) async-start(bf16[32,512,256]{1,2,0:T(8,128)(2,1)} %stack.2), calls=%async_computation | async-start | bytes 16777216 | tf_op jit(solution)/shard_map/all_to_all | solution.py:80
  24.0 358.1 %reduce-scatter.2.cloned.1.call-start = ((), (), s32[]{:S(2)}) async-start(), calls=%async_computation.2 | async-start | bytes 6684672 | tf_op jit(solution)/shard_map/reduce_scatter | solution.py:85
  24.1 180.0 %collective-permute-start = (bf16[3,2,512]{2,1,0:T(2,128)(2,1)S(1)}, bf16[3,2,512]{2,1,0:T(2,128)(2,1)S(1)}, u32[]{:S(2)}, u32[]{:S(2)}) collective-permute-start(bf16[3,2,512]{2,1,0:T(2,128)(2,1)S(1)} %slice.38), channel_id=1, source_target_pairs={{0,16},{16,32},{32,48},{48,64},{64,80},{80,96},{96,112},{112,128},... | collective-permute-start | bytes 18440 | tf_op jit(solution)/shard_map/ppermute | solution.py:14
  204.1 0.6 copy-start.3
  206.4 6.6 %collective-permute-start.1 = (bf16[127,512]{1,0:T(8,128)(2,1)S(1)}, bf16[127,512]{1,0:T(8,128)(2,1)S(1)}, u32[]{:S(2)}, u32[]{:S(2)}) collective-permute-start(bf16[127,512]{1,0:T(8,128)(2,1)S(1)} %slice_bitcast_fusion), channel_id=1, source_target_pairs={{0,16},{16,32},{32,48},{48,64},{64,80},{80,96},{96,112},{112,128},... | collective-permute-start | bytes 390152 | tf_op jit(solution)/shard_map/ppermute | solution.py:14
  214.2 9.3 %copy-start.4 = (f32[512]{0:T(512)S(1)}, f32[512]{0:T(512)}, u32[]{:S(2)}) copy-start(f32[512]{0:T(512)} %param.9) | copy-start | bytes 6148
  233.3 0.7 copy-start.5
  383.4 6.5 %collective-permute-start.2 = (bf16[64,512]{1,0:T(8,128)(2,1)S(1)}, bf16[64,512]{1,0:T(8,128)(2,1)S(1)}, u32[]{:S(2)}, u32[]{:S(2)}) collective-permute-start(bf16[64,512]{1,0:T(8,128)(2,1)S(1)} %constant_dynamic-slice_fusion.4), channel_id=1, source_target_pairs={{0,256},{16,272},{32,288},{48,304},{64,320},{80,336},{96,352},{112... | collective-permute-start | bytes 196616 | tf_op jit(solution)/shard_map/ppermute | solution.py:29
  390.0 8.6 %collective-permute-start.3 = (bf16[32,512]{1,0:T(8,128)(2,1)S(1)}, bf16[32,512]{1,0:T(8,128)(2,1)S(1)}, u32[]{:S(2)}, u32[]{:S(2)}) collective-permute-start(bf16[32,512]{1,0:T(8,128)(2,1)S(1)} %constant_dynamic-slice_fusion.3), channel_id=1, source_target_pairs={{0,128},{16,144},{32,160},{48,176},{64,192},{80,208},{96,224},{112... | collective-permute-start | bytes 98312 | tf_op jit(solution)/shard_map/ppermute | solution.py:29
  398.6 5.5 %collective-permute-start.4 = (bf16[16,512]{1,0:T(8,128)(2,1)S(1)}, bf16[16,512]{1,0:T(8,128)(2,1)S(1)}, u32[]{:S(2)}, u32[]{:S(2)}) collective-permute-start(bf16[16,512]{1,0:T(8,128)(2,1)S(1)} %constant_dynamic-slice_fusion.2), channel_id=1, source_target_pairs={{0,64},{16,80},{32,96},{48,112},{64,0},{80,16},{96,32},{112,48},{1... | collective-permute-start | bytes 49160 | tf_op jit(solution)/shard_map/ppermute | solution.py:29
  404.2 4.4 %collective-permute-start.5 = (bf16[8,512]{1,0:T(8,128)(2,1)S(1)}, bf16[8,512]{1,0:T(8,128)(2,1)S(1)}, u32[]{:S(2)}, u32[]{:S(2)}) collective-permute-start(bf16[8,512]{1,0:T(8,128)(2,1)S(1)} %constant_dynamic-slice_fusion.1), channel_id=1, source_target_pairs={{0,32},{16,48},{32,0},{48,16},{64,96},{80,112},{96,64},{112,80},{1... | collective-permute-start | bytes 24584 | tf_op jit(solution)/shard_map/ppermute | solution.py:29
  408.6 8.4 %collective-permute-start.6 = (bf16[4,512]{1,0:T(4,128)(2,1)S(1)}, bf16[4,512]{1,0:T(4,128)(2,1)S(1)}, u32[]{:S(2)}, u32[]{:S(2)}) collective-permute-start(bf16[4,512]{1,0:T(4,128)(2,1)S(1)} %constant_dynamic-slice_fusion), channel_id=1, source_target_pairs={{0,16},{16,0},{32,48},{48,32},{64,80},{80,64},{96,112},{112,96},{1... | collective-permute-start | bytes 12296 | tf_op jit(solution)/shard_map/ppermute | solution.py:29
Sparse Core Ops, SparseCore 0:
  233.4 148.6 reduce-scatter.1
